TPU v7x, 512 devices: a whole 4x8x8 slice. The times are simulated.
512 devices in a mesh: dp: 8 (over z_hi, core), seq: 64 (over x, z_lo, y).
Axes of the slice: x: 4, y: 8, z: 8 (z_hi: 4, z_lo: 2; z = z_hi * 2 + z_lo), core: 2. Of those that a mesh axis runs over, the one named last changes fastest.
Arguments:
- y_first: bfloat16 [8, 128, 64, 1152], P('dp', 'seq'), may hold values from -10 to 10
- y_second: bfloat16 [8, 128, 64, 1152], P('dp', 'seq'), may hold values from -10 to 10
- grad_first: bfloat16 [8, 128, 64, 1152], P('dp', 'seq'), may hold values from -6 to 6
- grad_second: bfloat16 [8, 128, 64, 1152], P('dp', 'seq'), may hold values from -6 to 6
- w_qkv_space: bfloat16 [1152, 1728], P('seq', 'dp'), may hold values from -1 to 1
- w_out_space: bfloat16 [576, 1152], P('seq', 'dp'), may hold values from -0.25 to 0.25
- w_qkv_time: bfloat16 [1152, 1728], P('seq', 'dp'), may hold values from -1 to 1
- w_out_time: bfloat16 [576, 1152], P('seq', 'dp'), may hold values from -0.25 to 0.25
Outputs:
- x_first: bfloat16 [8, 128, 64, 1152], P('dp', 'seq')
- x_second: bfloat16 [8, 128, 64, 1152], P('dp', 'seq')
- d_first: bfloat16 [8, 128, 64, 1152], P('dp', 'seq')
- d_second: bfloat16 [8, 128, 64, 1152], P('dp', 'seq')
- grad_w_out_time: float32 [576, 1152], P('seq', 'dp')
All inputs are finite; a program needn't handle non-finite values.
Results may differ from a plain program's by a relative error of at most 0.025.
Values may be sent and summed in bfloat16 or wider, within the bound.
No kernel may reach another device: no remote copies, remote signals or barrier semaphores. Data moves between devices by JAX's collectives and lax.ppermute only.
A program may use at most 64 MiB of HBM per device.

v0:
```python
import math
import jax
import jax.numpy as jnp
from jax import lax
from jax.sharding import PartitionSpec as P

HEADS = 8
HD = 72


def for_sending(shard):

    def short(part):
        return part.astype(jnp.bfloat16) if part.dtype == jnp.float32 else part

    return jax.tree.map(short, shard)


def normalize(values):
    wide = values.astype(jnp.float32)
    scale = lax.rsqrt(jnp.mean(wide * wide, axis=-1, keepdims=True) + 1e-06)
    return (wide * scale).astype(jnp.bfloat16)


def attend(inputs, w_qkv, w_out):
    outer, rows, inner, width = inputs.shape
    normed = normalize(inputs).reshape(-1, width)
    packed = jnp.dot(normed, w_qkv, preferred_element_type=jnp.float32).astype(jnp.bfloat16)
    packed = packed.reshape(outer, rows, inner, 3, HEADS, HD)
    query = packed[:, :, :, 0]
    keys = packed[:, :, :, 1]
    values = packed[:, :, :, 2]
    scores = jnp.einsum(
        "arbhk,asbhk->abhrs", query, keys, preferred_element_type=jnp.float32
    ) / math.sqrt(HD)
    peak = jnp.max(scores, axis=-1, keepdims=True)
    expo = jnp.exp(scores - peak)
    probs = (expo / jnp.sum(expo, axis=-1, keepdims=True)).astype(jnp.bfloat16)
    mixed = jnp.einsum(
        "abhrs,asbhk->arbhk", probs, values, preferred_element_type=jnp.float32
    ).astype(jnp.bfloat16)
    mixed = mixed.reshape(outer, rows, inner, HEADS * HD)
    result = jnp.dot(
        mixed.reshape(-1, HEADS * HD), w_out, preferred_element_type=jnp.float32
    ).astype(jnp.bfloat16)
    return (result.reshape(inputs.shape), mixed)


def body(
    y_first, y_second, grad_first, grad_second, w_qkv_space, w_out_space, w_qkv_time, w_out_time
):
    part_a, part_b, part_c, part_d = (
        lax.all_gather(w_qkv_space, "seq", axis=0, tiled=True),
        lax.all_gather(w_out_space, "seq", axis=0, tiled=True),
        lax.all_gather(w_qkv_time, "seq", axis=0, tiled=True),
        lax.all_gather(w_out_time, "seq", axis=0, tiled=True),
    )
    space_qkv, space_proj, time_qkv, time_proj = (
        lax.all_gather(part_a, "dp", axis=1, tiled=True),
        lax.all_gather(part_b, "dp", axis=1, tiled=True),
        lax.all_gather(part_c, "dp", axis=1, tiled=True),
        lax.all_gather(part_d, "dp", axis=1, tiled=True),
    )
    frame_count = y_first.shape[1]
    tokens = y_first.shape[2]
    width = y_first.shape[3]

    def time_fn(inputs):
        return attend(inputs, time_qkv, time_proj)

    def space_fn(inputs):
        return attend(inputs, space_qkv, space_proj)[0]

    first_patch = lax.all_to_all(y_first, "seq", split_axis=2, concat_axis=1, tiled=True)
    time_out, time_vjp, time_mixed = jax.vjp(time_fn, first_patch, has_aux=True)
    time_frames = jax.tree.map(
        lambda part, own: part.astype(own.dtype),
        lax.all_to_all(for_sending(time_out), "seq", split_axis=1, concat_axis=2, tiled=True),
        time_out,
    )
    second_in = (y_second.astype(jnp.float32) - time_frames.astype(jnp.float32)).astype(
        jnp.bfloat16
    )
    space_out, space_vjp = jax.vjp(space_fn, second_in.reshape(frame_count, tokens, 1, width))
    first_in = (
        y_first.astype(jnp.float32) - space_out.reshape(y_first.shape).astype(jnp.float32)
    ).astype(jnp.bfloat16)
    cot_patch = lax.all_to_all(grad_second, "seq", split_axis=2, concat_axis=1, tiled=True)
    back_patch = time_vjp(cot_patch)[0]
    back_frames = jax.tree.map(
        lambda part, own: part.astype(own.dtype),
        lax.all_to_all(for_sending(back_patch), "seq", split_axis=1, concat_axis=2, tiled=True),
        back_patch,
    )
    first_grad = (grad_first.astype(jnp.float32) + back_frames.astype(jnp.float32)).astype(
        jnp.bfloat16
    )
    back_space = space_vjp(first_grad.reshape(frame_count, tokens, 1, width))[0]
    second_grad = (
        grad_second.astype(jnp.float32) + back_space.reshape(y_first.shape).astype(jnp.float32)
    ).astype(jnp.bfloat16)
    partial_grad = lax.dot_general(
        time_mixed.reshape(-1, time_mixed.shape[3]),
        cot_patch.reshape(-1, width),
        (((0,), (0,)), ((), ())),
        preferred_element_type=jnp.float32,
    )
    row_share = lax.psum_scatter(partial_grad, "seq", scatter_dimension=0, tiled=True)
    grad_share = lax.psum_scatter(
        row_share.astype(jnp.bfloat16), "dp", scatter_dimension=1, tiled=True
    ).astype(jnp.float32)
    return (first_in, second_in, first_grad, second_grad, grad_share)


def solution(mesh):
    placed = (
        P("dp", "seq", None, None),
        P("dp", "seq", None, None),
        P("dp", "seq", None, None),
        P("dp", "seq", None, None),
        P("seq", "dp"),
        P("seq", "dp"),
        P("seq", "dp"),
        P("seq", "dp"),
    )
    return jax.shard_map(
        body,
        mesh=mesh,
        in_specs=placed,
        out_specs=(
            P("dp", "seq", None, None),
            P("dp", "seq", None, None),
            P("dp", "seq", None, None),
            P("dp", "seq", None, None),
            P("seq", "dp"),
        ),
        check_vma=False,
    )
```

profile of v0, /device:TPU:1, one launch (start us, length us, event | category | flops | bytes accessed | tf_op | source)
XLA Modules:
  0.0 1113.6 jit_solution(6876074772628245804)
XLA Ops:
  7.2 133.8 %all-gather.1 = bf16[64,9,144]{2,1,0:T(8,128)(2,1)S(1)} all-gather(bf16[1,9,144]{2,1,0:T(8,128)(2,1)} %bitcast.214), channel_id=1, replica_groups=mesh['dp'=8,'seq'=64] {'seq'}, dimensions={0}, use_global_device_ids=true | all-gather | bytes 168480 | tf_op jit(solution)/shard_map/all_gather | solution.py:56
  142.1 127.3 %all-gather = bf16[64,18,216]{2,1,0:T(8,128)(2,1)S(1)} all-gather(bf16[1,18,216]{2,1,0:T(8,128)(2,1)} %bitcast.212), channel_id=1, replica_groups=mesh['dp'=8,'seq'=64] {'seq'}, dimensions={0}, use_global_device_ids=true | all-gather | bytes 505440 | tf_op jit(solution)/shard_map/all_gather | solution.py:55
  271.8 4.6 all-to-all-start
  279.4 8.3 all-to-all-done
  287.7 4.6 all-to-all-start.2
  293.8 9.9 all-to-all-done.2
  303.8 2.0 convolution_convert_fusion.17
  305.8 75.2 %all-gather.9.cloned.1.call-done = bf16[1152,1728]{0,1:T(8,128)(2,1)} async-done(((bf16[1152,216]{0,1:T(8,128)(2,1)}), bf16[1152,1728]{0,1:T(8,128)(2,1)}) %all-gather.9.cloned.1.call-update) | async-done | bytes 3981328 | tf_op jit(solution)/shard_map/all_gather | solution.py:61
  381.0 3.4 convolution_convert_fusion.3
  384.8 1.6 convert_reduce_fusion.1
  389.3 287.2 %all-reduce.8 = bf16[576,1152]{1,0:T(8,128)(2,1)} all-reduce(f32[576,1152]{1,0:T(8,128)S(1)} %fusion.60), channel_id=2, replica_groups=mesh['dp'=8,'seq'=64] {'seq'}, use_global_device_ids=true, to_apply=%region_14.0.clone | all-reduce | flops 663552 | bytes 3981312
  678.3 125.7 %all-gather.3 = bf16[64,9,144]{2,1,0:T(8,128)(2,1)S(1)} all-gather(bf16[1,9,144]{2,1,0:T(8,128)(2,1)} %bitcast.215), channel_id=1, replica_groups=mesh['dp'=8,'seq'=64] {'seq'}, dimensions={0}, use_global_device_ids=true | all-gather | bytes 168480 | tf_op jit(solution)/shard_map/all_gather | solution.py:54
  805.1 129.5 %all-gather.2 = bf16[64,18,216]{2,1,0:T(8,128)(2,1)S(1)} all-gather(bf16[1,18,216]{2,1,0:T(8,128)(2,1)S(1)} %bitcast.213), channel_id=1, replica_groups=mesh['dp'=8,'seq'=64] {'seq'}, dimensions={0}, use_global_device_ids=true | all-gather | bytes 505440 | tf_op jit(solution)/shard_map/all_gather | solution.py:53
  937.0 3.0 multiply_reduce_fusion
  941.3 2.4 reduce.29
  944.5 4.6 all-to-all-start.3
  950.2 2.4 reduce.28
  954.9 5.3 all-to-all-done.3
  960.3 5.6 all-to-all-start.1
  966.9 2.2 convolution_convert_fusion.16
  969.5 7.3 all-to-all-done.1
  978.0 115.5 %all-gather.13.cloned.1.call-done = bf16[1152,1728]{0,1:T(8,128)(2,1)} async-done(((bf16[1152,216]{0,1:T(8,128)(2,1)}), bf16[1152,1728]{0,1:T(8,128)(2,1)}) %all-gather.13.cloned.1.call-update) | async-done | bytes 3981328 | tf_op jit(solution)/shard_map/all_gather | solution.py:59
  1093.5 3.3 convolution_convert_fusion.2
  1101.8 3.0 fusion
  (145 shorter events, 30.7 us)
Async XLA Ops:
  7.2 296.6 %all-gather.11.cloned.1.call-start = ((), (), s32[]{:S(2)}) async-start(), calls=%async_computation.6 | async-start | bytes 1658880 | tf_op jit(solution)/shard_map/all_gather | solution.py:62
  141.0 129.8 %copy-start.10 = (bf16[1,2,64,1152]{3,2,1,0:T(8,128)(2,1)S(1)}, bf16[1,2,64,1152]{3,2,1,0:T(8,128)(2,1)}, u32[]{:S(2)}) copy-start(bf16[1,2,64,1152]{3,2,1,0:T(8,128)(2,1)} %param.8) | copy-start | bytes 884740
  142.0 134.4 %copy-start.12 = (bf16[1,2,64,1152]{3,2,1,0:T(8,128)(2,1)S(1)}, bf16[1,2,64,1152]{3,2,1,0:T(8,128)(2,1)}, u32[]{:S(2)}) copy-start(bf16[1,2,64,1152]{3,2,1,0:T(8,128)(2,1)} %param.11) | copy-start | bytes 884740
  142.0 239.0 %all-gather.9.cloned.1.call-start = ((), (), s32[]{:S(2)}) async-start(), calls=%async_computation.5 | async-start | bytes 4478976 | tf_op jit(solution)/shard_map/all_gather | solution.py:61
  271.8 15.9 %all-to-all-start = ((bf16[1,2,64,1152]{3,1,0,2:T(2,128)(2,1)}), bf16[1,2,64,1152]{3,1,0,2:T(2,128)(2,1)S(1)}, u32[]{:S(2)}, u32[]{:S(2)}) async-start(bf16[1,2,64,1152]{3,1,0,2:T(2,128)(2,1)} %copy.132), calls=%async_computation | async-start | bytes 589824 | tf_op jit(solution)/shard_map/all_to_all | solution.py:74
  287.7 15.9 %all-to-all-start.2 = ((bf16[1,2,64,1152]{3,1,0,2:T(2,128)(2,1)}), bf16[1,2,64,1152]{3,1,0,2:T(2,128)(2,1)S(1)}, u32[]{:S(2)}, u32[]{:S(2)}) async-start(bf16[1,2,64,1152]{3,1,0,2:T(2,128)(2,1)} %copy.148), calls=%async_computation.2 | async-start | bytes 589824 | tf_op jit(solution)/shard_map/all_to_all | solution.py:88
  292.3 661.1 %reduce-scatter.4.cloned.1.call-start = ((), (), s32[]{:S(2)}) async-start(), calls=%async_computation.9 | async-start | bytes 331776
  293.7 90.7 %copy-start.22 = (f32[128]{0:T(128)}, f32[128]{0:T(128)S(1)}, u32[]{:S(2)}) copy-start(f32[128]{0:T(128)S(1)} %rsqrt.26) | copy-start | bytes 1540
  305.8 79.0 %copy-start.15 = (bf16[128,576]{0,1:T(8,128)(2,1)}, bf16[128,576]{0,1:T(8,128)(2,1)S(1)}, u32[]{:S(2)}) copy-start(bf16[128,576]{0,1:T(8,128)(2,1)S(1)} %convolution_convert_fusion.17) | copy-start | bytes 442372
  389.3 415.9 %copy-start.20 = (bf16[18,216]{1,0:T(8,128)(2,1)S(1)}, bf16[18,216]{1,0:T(8,128)(2,1)}, u32[]{:S(2)}) copy-start(bf16[18,216]{1,0:T(8,128)(2,1)} %param.12) | copy-start | bytes 23332
  678.2 288.6 %all-gather.15.cloned.1.call-start = ((), (), s32[]{:S(2)}) async-start(), calls=%async_computation.8 | async-start | bytes 1658880 | tf_op jit(solution)/shard_map/all_gather | solution.py:60
  804.0 132.1 %copy-start.7 = (bf16[8,128,128]{1,2,0:T(8,128)(2,1)S(1)}, bf16[8,128,128]{1,2,0:T(8,128)(2,1)}, u32[]{:S(2)}) copy-start(bf16[8,128,128]{1,2,0:T(8,128)(2,1)} %copy-done.6) | copy-start | bytes 786436
  804.0 132.1 %copy-start.16 = (bf16[128,576]{0,1:T(8,128)(2,1)S(1)}, bf16[128,576]{0,1:T(8,128)(2,1)}, u32[]{:S(2)}) copy-start(bf16[128,576]{0,1:T(8,128)(2,1)} %copy-done.15) | copy-start | bytes 442372
  804.2 132.1 %copy-start.21 = (f32[8,128]{1,0:T(8,128)S(1)}, f32[8,128]{1,0:T(8,128)}, u32[]{:S(2)}) copy-start(f32[8,128]{1,0:T(8,128)} %get-tuple-element.11) | copy-start | bytes 12292
  804.2 132.2 %copy-start.2 = (f32[8,128,128]{1,2,0:T(8,128)S(1)}, f32[8,128,128]{1,2,0:T(8,128)}, u32[]{:S(2)}) copy-start(f32[8,128,128]{1,2,0:T(8,128)} %get-tuple-element.10) | copy-start | bytes 1572868
  804.2 132.2 %copy-start.5 = (bf16[128,1728]{0,1:T(8,128)(2,1)S(1)}, bf16[128,1728]{0,1:T(8,128)(2,1)}, u32[]{:S(2)}) copy-start(bf16[128,1728]{0,1:T(8,128)(2,1)} %copy-done.4) | copy-start | bytes 1327108
  804.2 132.2 %copy-start.17 = (pred[8,128,128]{1,2,0:T(32,128)(4,1)S(1)}, pred[8,128,128]{1,2,0:T(32,128)(4,1)}, u32[]{:S(2)}) copy-start(pred[8,128,128]{1,2,0:T(32,128)(4,1)} %get-tuple-element.12) | copy-start | bytes 393220
  805.1 288.4 %all-gather.13.cloned.1.call-start = ((), (), s32[]{:S(2)}) async-start(), calls=%async_computation.7 | async-start | bytes 4478976 | tf_op jit(solution)/shard_map/all_gather | solution.py:59
  944.5 15.8 %all-to-all-start.3 = ((bf16[64,2,1152]{2,1,0:T(2,128)(2,1)}), bf16[64,2,1152]{2,1,0:T(2,128)(2,1)S(1)}, u32[]{:S(2)}, u32[]{:S(2)}) async-start(bf16[64,2,1152]{2,1,0:T(2,128)(2,1)} %reshape.522), calls=%async_computation.3 | async-start | bytes 589824 | tf_op jit(solution)/shard_map/all_to_all | solution.py:92
  949.8 17.0 %copy-start.18 = (bf16[1,2,64,1152]{3,2,1,0:T(8,128)(2,1)S(1)}, bf16[1,2,64,1152]{3,2,1,0:T(8,128)(2,1)}, u32[]{:S(2)}) copy-start(bf16[1,2,64,1152]{3,2,1,0:T(8,128)(2,1)} %param.10) | copy-start | bytes 884740
  960.3 16.5 %all-to-all-start.1 = ((bf16[64,2,1152]{2,1,0:T(2,128)(2,1)}), bf16[64,2,1152]{2,1,0:T(2,128)(2,1)S(1)}, u32[]{:S(2)}, u32[]{:S(2)}) async-start(bf16[64,2,1152]{2,1,0:T(2,128)(2,1)} %reshape.520), calls=%async_computation.1 | async-start | bytes 589824 | tf_op jit(solution)/shard_map/all_to_all | solution.py:78
  966.8 11.0 copy-start.14
  966.8 10.8 copy-start.19
  977.8 128.1 %copy-start.3 = (bf16[1,2,64,1152]{3,2,1,0:T(8,128)(2,1)}, bf16[1,2,64,1152]{3,2,1,0:T(8,128)(2,1)S(1)}, u32[]{:S(2)}) copy-start(bf16[1,2,64,1152]{3,2,1,0:T(8,128)(2,1)S(1)} %get-tuple-element.14) | copy-start | bytes 884740
  (11 other events, 44.7 us)
Sparse Core Ops, SparseCore 0:
  142.2 59.9 all-gather.10
  270.9 110.1 all-gather.8
  678.4 83.5 reduce-scatter.3
  805.2 108.5 all-gather.14
  936.1 157.3 all-gather.12
where the time goes:
time: 1110 us
  blocking collectives  803 us (72%)
  waiting for transfers between devices  222 us (20%)
  matrix products  23.2 us (2%)
  local copies, waits for them, and re-layouts  19.8 us (2%)
  starting transfers between devices  19.7 us (2%)
  between operations  15.2 us (1%)
    unnamed x1, blocking collectives  287 us
    all_gather x1, blocking collectives, body(): lax.all_gather(w_out_time, 'seq', axis=0, tiled=True)  134 us
    all_gather x1, blocking collectives, body(): lax.all_gather(w_qkv_space, 'seq', axis=0, tiled=True)  130 us
    all_gather x1, blocking collectives, body(): lax.all_gather(w_qkv_time, 'seq', axis=0, tiled=True)  127 us
    all_gather x1, blocking collectives, body(): lax.all_gather(w_out_space, 'seq', axis=0, tiled=True)  126 us
    all_gather x1, waiting for transfers between devices, body(): lax.all_gather(part_a, 'dp', axis=1, tiled=True)  115 us
    all_gather x1, waiting for transfers between devices, body(): lax.all_gather(part_c, 'dp', axis=1, tiled=True)  75.2 us
  transfers between devices with their start and end apart: 9, of which 6 were waited for; matrix products, arithmetic and copies ran while one was open for 3% of the time, Pallas kernels for 0%

commit v1 on v0

--- a/solution.py
+++ b/solution.py
@@ -6,6 +6,12 @@
 
 HEADS = 8
 HD = 72
+
+
+def form_plane(a0):
+    return jnp.concatenate(
+        lax.all_to_all(jnp.stack(lax.axis_size("seq") * [a0], axis=0), "seq", 0, 0), axis=0
+    )
 
 
 def for_sending(shard):
@@ -52,7 +58,7 @@
     part_a, part_b, part_c, part_d = (
         lax.all_gather(w_qkv_space, "seq", axis=0, tiled=True),
         lax.all_gather(w_out_space, "seq", axis=0, tiled=True),
-        lax.all_gather(w_qkv_time, "seq", axis=0, tiled=True),
+        form_plane(w_qkv_time),
         lax.all_gather(w_out_time, "seq", axis=0, tiled=True),
     )
     space_qkv, space_proj, time_qkv, time_proj = (

time: 1110 us -> 998 us (0.90)
  blocking collectives: 803 us -> 692 us
    all_gather x1 -> x0, blocking collectives: 127 us -> none  [body(): lax.all_gather(w_qkv_time, 'seq', axis=0, tiled=True)]
    all_gather x1, waiting for transfers between devices: 75.2 us -> 55.6 us  [body(): lax.all_gather(part_c, 'dp', axis=1, tiled=True)]
    all_to_all x0 -> x1, blocking collectives: none -> 19.4 us  [form_plane(): lax.all_to_all(jnp.stack(lax.axis_size('seq') * [a0], axis=0), 'seq', 0, 0)]
  transfers between devices with their start and end apart: 9 -> 9, of which waited for: 6 -> 7; matrix products, arithmetic and copies ran while one was open for 3% -> 3% of each run, Pallas kernels for 0% -> 0%
where the time goes in v1:
time: 998 us; the launch traced here: 997 us
  blocking collectives  692 us (69%)
  waiting for transfers between devices  215 us (22%)
  matrix products  23.2 us (2%)
  starting transfers between devices  20.6 us (2%)
  local copies, waits for them, and re-layouts  20.6 us (2%)
  between operations  15.2 us (2%)
  other arithmetic  10.6 us (1%)
    unnamed x1, blocking collectives  284 us
    all_gather x1, blocking collectives, body(): lax.all_gather(w_out_time, 'seq', axis=0, tiled=True)  134 us
    all_gather x1, blocking collectives, body(): lax.all_gather(w_qkv_space, 'seq', axis=0, tiled=True)  129 us
    all_gather x1, blocking collectives, body(): lax.all_gather(w_out_space, 'seq', axis=0, tiled=True)  126 us
    all_gather x1, waiting for transfers between devices, body(): lax.all_gather(part_a, 'dp', axis=1, tiled=True)  119 us
    all_gather x1, waiting for transfers between devices, body(): lax.all_gather(part_c, 'dp', axis=1, tiled=True)  55.6 us
  transfers between devices with their start and end apart: 9, of which 7 were waited for; matrix products, arithmetic and copies ran while one was open for 3% of the time, Pallas kernels for 0%

profile of v1, /device:TPU:1, one launch (start us, length us, event | category | flops | bytes accessed | tf_op | source)
XLA Modules:
  0.0 996.9 jit_solution(8830713037729927957)
XLA Ops:
  7.2 133.8 %all-gather = bf16[64,9,144]{2,1,0:T(8,128)(2,1)S(1)} all-gather(bf16[1,9,144]{2,1,0:T(8,128)(2,1)} %bitcast.212), channel_id=1, replica_groups=mesh['dp'=8,'seq'=64] {'seq'}, dimensions={0}, use_global_device_ids=true | all-gather | bytes 168480 | tf_op jit(solution)/shard_map/all_gather | solution.py:62
  142.9 19.4 %all_to_all.47 = bf16[64,18,216]{2,1,0:T(8,128)(2,1)S(1)} all-to-all(bf16[64,18,216]{2,1,0:T(8,128)(2,1)S(1)} %stack.2), channel_id=1, replica_groups=mesh['dp'=8,'seq'=64] {'seq'}, dimensions={0} | all-to-all | bytes 995328 | tf_op jit(solution)/shard_map/all_to_all | solution.py:13
  164.7 5.6 all-to-all-start
  173.3 8.3 all-to-all-done
  181.6 4.6 all-to-all-start.3
  187.7 9.8 all-to-all-done.3
  197.6 9.0 all-gather.10.cloned.1.call-done
  206.6 2.0 convolution_convert_fusion.17
  208.7 55.6 %all-gather.8.cloned.1.call-done = bf16[1152,1728]{0,1:T(8,128)(2,1)} async-done(((bf16[1152,216]{0,1:T(8,128)(2,1)}), bf16[1152,1728]{0,1:T(8,128)(2,1)}) %all-gather.8.cloned.1.call-update) | async-done | bytes 3981328 | tf_op jit(solution)/shard_map/all_gather | solution.py:67
  264.3 3.4 convolution_convert_fusion.3
  272.6 284.1 %all-reduce.8 = bf16[576,1152]{1,0:T(8,128)(2,1)} all-reduce(f32[576,1152]{1,0:T(8,128)S(1)} %fusion.60), channel_id=2, replica_groups=mesh['dp'=8,'seq'=64] {'seq'}, use_global_device_ids=true, to_apply=%region_14.0.clone | all-reduce | flops 663552 | bytes 3981312
  558.5 125.6 %all-gather.2 = bf16[64,9,144]{2,1,0:T(8,128)(2,1)S(1)} all-gather(bf16[1,9,144]{2,1,0:T(8,128)(2,1)} %bitcast.213), channel_id=1, replica_groups=mesh['dp'=8,'seq'=64] {'seq'}, dimensions={0}, use_global_device_ids=true | all-gather | bytes 168480 | tf_op jit(solution)/shard_map/all_gather | solution.py:60
  685.2 128.9 %all-gather.1 = bf16[64,18,216]{2,1,0:T(8,128)(2,1)S(1)} all-gather(bf16[1,18,216]{2,1,0:T(8,128)(2,1)S(1)} %bitcast.211), channel_id=1, replica_groups=mesh['dp'=8,'seq'=64] {'seq'}, dimensions={0}, use_global_device_ids=true | all-gather | bytes 505440 | tf_op jit(solution)/shard_map/all_gather | solution.py:59
  816.5 3.0 multiply_reduce_fusion
  820.7 2.4 reduce.29
  823.9 4.6 all-to-all-start.4
  829.6 2.4 reduce.28
  834.3 5.4 all-to-all-done.4
  839.8 5.5 all-to-all-start.2
  846.3 2.2 convolution_convert_fusion.16
  848.9 7.5 all-to-all-done.2
  857.7 119.2 %all-gather.12.cloned.1.call-done = bf16[1152,1728]{0,1:T(8,128)(2,1)} async-done(((bf16[1152,216]{0,1:T(8,128)(2,1)}), bf16[1152,1728]{0,1:T(8,128)(2,1)}) %all-gather.12.cloned.1.call-update) | async-done | bytes 3981328 | tf_op jit(solution)/shard_map/all_gather | solution.py:65
  976.9 3.3 convolution_convert_fusion.2
  985.1 3.0 fusion
  (146 shorter events, 33.1 us)
Async XLA Ops:
  7.2 199.4 %all-gather.10.cloned.1.call-start = ((), (), s32[]{:S(2)}) async-start(), calls=%async_computation.7 | async-start | bytes 1658880 | tf_op jit(solution)/shard_map/all_gather | solution.py:68
  142.0 21.7 %copy-start.10 = (bf16[1,2,64,1152]{3,2,1,0:T(8,128)(2,1)S(1)}, bf16[1,2,64,1152]{3,2,1,0:T(8,128)(2,1)}, u32[]{:S(2)}) copy-start(bf16[1,2,64,1152]{3,2,1,0:T(8,128)(2,1)} %param.8) | copy-start | bytes 884740
  142.1 122.2 %all-gather.8.cloned.1.call-start = ((), (), s32[]{:S(2)}) async-start(), calls=%async_computation.6 | async-start | bytes 4478976 | tf_op jit(solution)/shard_map/all_gather | solution.py:67
  142.9 27.5 %copy-start.12 = (bf16[1,2,64,1152]{3,2,1,0:T(8,128)(2,1)S(1)}, bf16[1,2,64,1152]{3,2,1,0:T(8,128)(2,1)}, u32[]{:S(2)}) copy-start(bf16[1,2,64,1152]{3,2,1,0:T(8,128)(2,1)} %param.11) | copy-start | bytes 884740
  164.7 16.9 %all-to-all-start = ((bf16[1,2,64,1152]{3,1,0,2:T(2,128)(2,1)}), bf16[1,2,64,1152]{3,1,0,2:T(2,128)(2,1)S(1)}, u32[]{:S(2)}, u32[]{:S(2)}) async-start(bf16[1,2,64,1152]{3,1,0,2:T(2,128)(2,1)} %copy.132), calls=%async_computation | async-start | bytes 589824 | tf_op jit(solution)/shard_map/all_to_all | solution.py:80
  181.6 15.9 %all-to-all-start.3 = ((bf16[1,2,64,1152]{3,1,0,2:T(2,128)(2,1)}), bf16[1,2,64,1152]{3,1,0,2:T(2,128)(2,1)S(1)}, u32[]{:S(2)}, u32[]{:S(2)}) async-start(bf16[1,2,64,1152]{3,1,0,2:T(2,128)(2,1)} %copy.148), calls=%async_computation.3 | async-start | bytes 589824 | tf_op jit(solution)/shard_map/all_to_all | solution.py:94
  186.2 646.6 %reduce-scatter.4.cloned.1.call-start = ((), (), s32[]{:S(2)}) async-start(), calls=%async_computation.10 | async-start | bytes 331776
  187.6 80.0 %copy-start.22 = (f32[128]{0:T(128)}, f32[128]{0:T(128)S(1)}, u32[]{:S(2)}) copy-start(f32[128]{0:T(128)S(1)} %rsqrt.26) | copy-start | bytes 1540
  208.7 59.5 %copy-start.15 = (bf16[128,576]{0,1:T(8,128)(2,1)}, bf16[128,576]{0,1:T(8,128)(2,1)S(1)}, u32[]{:S(2)}) copy-start(bf16[128,576]{0,1:T(8,128)(2,1)S(1)} %convolution_convert_fusion.17) | copy-start | bytes 442372
  272.6 412.7 %copy-start.20 = (bf16[18,216]{1,0:T(8,128)(2,1)S(1)}, bf16[18,216]{1,0:T(8,128)(2,1)}, u32[]{:S(2)}) copy-start(bf16[18,216]{1,0:T(8,128)(2,1)} %param.12) | copy-start | bytes 23332
  558.4 287.9 %all-gather.14.cloned.1.call-start = ((), (), s32[]{:S(2)}) async-start(), calls=%async_computation.9 | async-start | bytes 1658880 | tf_op jit(solution)/shard_map/all_gather | solution.py:66
  684.0 131.4 %copy-start.7 = (bf16[8,128,128]{1,2,0:T(8,128)(2,1)S(1)}, bf16[8,128,128]{1,2,0:T(8,128)(2,1)}, u32[]{:S(2)}) copy-start(bf16[8,128,128]{1,2,0:T(8,128)(2,1)} %copy-done.6) | copy-start | bytes 786436
  684.0 131.4 %copy-start.16 = (bf16[128,576]{0,1:T(8,128)(2,1)S(1)}, bf16[128,576]{0,1:T(8,128)(2,1)}, u32[]{:S(2)}) copy-start(bf16[128,576]{0,1:T(8,128)(2,1)} %copy-done.15) | copy-start | bytes 442372
  684.3 131.5 %copy-start.21 = (f32[8,128]{1,0:T(8,128)S(1)}, f32[8,128]{1,0:T(8,128)}, u32[]{:S(2)}) copy-start(f32[8,128]{1,0:T(8,128)} %get-tuple-element.11) | copy-start | bytes 12292
  684.3 131.5 %copy-start.2 = (f32[8,128,128]{1,2,0:T(8,128)S(1)}, f32[8,128,128]{1,2,0:T(8,128)}, u32[]{:S(2)}) copy-start(f32[8,128,128]{1,2,0:T(8,128)} %get-tuple-element.10) | copy-start | bytes 1572868
  684.3 131.5 %copy-start.5 = (bf16[128,1728]{0,1:T(8,128)(2,1)S(1)}, bf16[128,1728]{0,1:T(8,128)(2,1)}, u32[]{:S(2)}) copy-start(bf16[128,1728]{0,1:T(8,128)(2,1)} %copy-done.4) | copy-start | bytes 1327108
  684.3 131.5 %copy-start.17 = (pred[8,128,128]{1,2,0:T(32,128)(4,1)S(1)}, pred[8,128,128]{1,2,0:T(32,128)(4,1)}, u32[]{:S(2)}) copy-start(pred[8,128,128]{1,2,0:T(32,128)(4,1)} %get-tuple-element.12) | copy-start | bytes 393220
  685.2 291.7 %all-gather.12.cloned.1.call-start = ((), (), s32[]{:S(2)}) async-start(), calls=%async_computation.8 | async-start | bytes 4478976 | tf_op jit(solution)/shard_map/all_gather | solution.py:65
  823.9 15.9 %all-to-all-start.4 = ((bf16[64,2,1152]{2,1,0:T(2,128)(2,1)}), bf16[64,2,1152]{2,1,0:T(2,128)(2,1)S(1)}, u32[]{:S(2)}, u32[]{:S(2)}) async-start(bf16[64,2,1152]{2,1,0:T(2,128)(2,1)} %reshape.526), calls=%async_computation.4 | async-start | bytes 589824 | tf_op jit(solution)/shard_map/all_to_all | solution.py:98
  829.2 17.0 %copy-start.18 = (bf16[1,2,64,1152]{3,2,1,0:T(8,128)(2,1)S(1)}, bf16[1,2,64,1152]{3,2,1,0:T(8,128)(2,1)}, u32[]{:S(2)}) copy-start(bf16[1,2,64,1152]{3,2,1,0:T(8,128)(2,1)} %param.10) | copy-start | bytes 884740
  839.8 16.6 %all-to-all-start.2 = ((bf16[64,2,1152]{2,1,0:T(2,128)(2,1)}), bf16[64,2,1152]{2,1,0:T(2,128)(2,1)S(1)}, u32[]{:S(2)}, u32[]{:S(2)}) async-start(bf16[64,2,1152]{2,1,0:T(2,128)(2,1)} %reshape.524), calls=%async_computation.2 | async-start | bytes 589824 | tf_op jit(solution)/shard_map/all_to_all | solution.py:84
  846.2 11.2 %copy-start.14 = (bf16[1,2,64,1152]{3,2,1,0:T(8,128)(2,1)}, bf16[1,2,64,1152]{3,2,1,0:T(8,128)(2,1)S(1)}, u32[]{:S(2)}) copy-start(bf16[1,2,64,1152]{3,2,1,0:T(8,128)(2,1)S(1)} %fusion.15) | copy-start | bytes 884740
  846.2 11.0 %copy-start.19 = (bf16[1,2,64,1152]{3,2,1,0:T(8,128)(2,1)S(1)}, bf16[1,2,64,1152]{3,2,1,0:T(8,128)(2,1)}, u32[]{:S(2)}) copy-start(bf16[1,2,64,1152]{3,2,1,0:T(8,128)(2,1)} %param.9) | copy-start | bytes 884740
  857.5 131.8 %copy-start.3 = (bf16[1,2,64,1152]{3,2,1,0:T(8,128)(2,1)}, bf16[1,2,64,1152]{3,2,1,0:T(8,128)(2,1)S(1)}, u32[]{:S(2)}) copy-start(bf16[1,2,64,1152]{3,2,1,0:T(8,128)(2,1)S(1)} %get-tuple-element.14) | copy-start | bytes 884740
  (11 other events, 44.7 us)
Sparse Core Ops, SparseCore 0:
  142.2 64.4 all-gather.9
  208.8 55.4 all-gather.7
  558.5 86.4 reduce-scatter.3
  685.3 111.4 all-gather.13
  815.6 161.2 all-gather.11
